TPU v7x, 32 devices: a whole 2x2x4 slice. The times are simulated.
32 devices in a mesh: region: 4 (over z), narrow: 8 (over y, x, core).
Axes of the slice: x: 2, y: 2, z: 4, core: 2. Of those that a mesh axis runs over, the one named last changes fastest.
Arguments:
- dust_pos: float32 [3, 6144], P(None, ('region', 'narrow')), may hold values from -1 to 1
- dust_vel: float32 [3, 6144], P(None, ('region', 'narrow')), may hold values from -6 to 6
- dust_tau: float32 [6144], P(('region', 'narrow')), may hold values from 0.02 to 2
- dest: int32 [6144, 1], P(('region', 'narrow')), may hold values from 0 to 3; in each aligned block of 192 rows (0 to 191, 192 to 383, ...) at most 96 rows name the same one
- counts: int32 [32], P(('region', 'narrow')), may hold values from 96 to 192, as said below
- wake_pos: float32 [3, 32768], P(None, ('region', 'narrow')), may hold values from -1 to 1
- wake_gamma: float32 [3, 32768], P(None, ('region', 'narrow')), may hold values from -0.3 to 0.3
- wake_core: float32 [32768], P(('region', 'narrow')), may hold values from 0.05 to 0.3
Outputs:
- moved: float32 [6, 12288], P(None, ('region', 'narrow'))
Inputs may be any that keep to these rules, and one draw needn't show every extreme that they name: `dest`: in each device's 192 rows, no region is named by more than 96 rows, and some device's rows name some region exactly 96 times. `counts`: some device has all its rows live in every draw.
All inputs are finite; a program needn't handle non-finite values.
Results may differ from a plain program's by a relative error of at most 0.0003.
Values sent between devices are 32-bit elements; how exact they have to be, the bound alone decides.
No kernel may reach another device: no remote copies, remote signals or barrier semaphores. Data moves between devices by JAX's collectives and lax.ppermute only.
A program may use at most 64 MiB of HBM per device.

v0:
```python
import math
import jax
import jax.numpy as jnp
from jax import lax
from jax.sharding import PartitionSpec as P

step_size = 0.1
gravity = 1.0


def cross_rows(first, second):
    return jnp.stack(
        [
            first[1] * second[2] - first[2] * second[1],
            first[2] * second[0] - first[0] * second[2],
            first[0] * second[1] - first[1] * second[0],
        ]
    )


def raw_terms(points, wake_block):
    point_count = points.shape[1]
    wake_count = wake_block.shape[1]
    wake_width = math.gcd(wake_count, 2048)
    wake_place = wake_block[0:3]
    vortex_gamma = wake_block[3:6]
    core_square = wake_block[6] * wake_block[6]
    tables = jnp.concatenate([vortex_gamma, cross_rows(vortex_gamma, wake_place)], axis=0)
    place_blocks = wake_place.reshape(3, wake_count // wake_width, wake_width).transpose(1, 0, 2)
    table_blocks = tables.reshape(6, wake_count // wake_width, wake_width).transpose(1, 0, 2)
    core_blocks = core_square.reshape(wake_count // wake_width, wake_width)
    point_blocks = points.reshape(3, point_count // point_count, point_count).transpose(1, 0, 2)

    def one_block(point_group):

        def accumulate(running, parts):
            place_part, table_part, core_part = parts
            first_gap = point_group[0][:, None] - place_part[0][None, :]
            second_gap = point_group[1][:, None] - place_part[1][None, :]
            third_gap = point_group[2][:, None] - place_part[2][None, :]
            distance_sq = (
                first_gap * first_gap
                + second_gap * second_gap
                + third_gap * third_gap
                + core_part[None, :]
            )
            inverse_root = lax.rsqrt(distance_sq)
            kernel = inverse_root * inverse_root * inverse_root
            product = lax.dot_general(
                table_part, kernel, (((1,), (1,)), ((), ())), precision=lax.Precision.HIGH
            )
            return (running + product, None)

        total, _ = lax.scan(
            accumulate,
            jnp.zeros((6, point_count), jnp.float32),
            (place_blocks, table_blocks, core_blocks),
        )
        return total

    result = lax.map(one_block, point_blocks)
    return result.transpose(1, 0, 2).reshape(6, point_count)


def advance(arrived, raw_sums):
    points = arrived[0:3]
    velocity = arrived[3:6]
    live_flag = arrived[7]
    wind = (cross_rows(raw_sums[0:3], points) - raw_sums[3:6]) / (4.0 * math.pi)
    safe_tau = jnp.where(live_flag > 0.5, arrived[6], 1.0)
    rate = step_size / safe_tau
    upward = jnp.array([0.0, 0.0, 1.0], jnp.float32)[:, None]
    new_velocity = (velocity + rate[None, :] * wind - step_size * gravity * upward) / (
        1.0 + rate[None, :]
    )
    new_place = points + step_size * new_velocity
    return jnp.concatenate([new_place, new_velocity], axis=0) * live_flag[None, :]


def exchange_slots(outgoing, capacity):
    regions = lax.axis_size("region")
    if regions > 8:
        return lax.all_to_all(outgoing, "region", split_axis=1, concat_axis=1, tiled=True)
    region = lax.axis_index("region")
    blocks = outgoing.reshape(outgoing.shape[0], regions, capacity)
    by_shift = [jnp.take(blocks, region, axis=1)]
    for shift in range(1, regions):
        pairs = [(i, (i + shift) % regions) for i in range(regions)]
        sent = jnp.take(blocks, (region + shift) % regions, axis=1)
        by_shift.append(lax.ppermute(sent, "region", pairs))
    stacked = jnp.stack(by_shift, axis=1)
    order = (region - jnp.arange(regions, dtype=jnp.int32)) % regions
    return jnp.take(stacked, order, axis=1).reshape(outgoing.shape[0], regions * capacity)


def body(dust_pos, dust_vel, dust_tau, dest, counts, wake_pos, wake_gamma, wake_core):
    per_device = dust_tau.shape[0]
    regions = lax.axis_size("region")
    capacity = 2 * per_device // regions
    slot_count = regions * capacity
    live_rows = (jnp.arange(per_device, dtype=jnp.int32) < counts[0]).astype(jnp.float32)
    target = dest[:, 0]
    row = jnp.arange(per_device, dtype=jnp.int32)
    earlier = (target[:, None] == target[None, :]) & (row[None, :] < row[:, None])
    slot_rank = jnp.sum(earlier.astype(jnp.int32), axis=1)
    column = target * capacity + slot_rank
    placing = (column[:, None] == jnp.arange(slot_count, dtype=jnp.int32)[None, :]).astype(
        jnp.float32
    )
    dust_state = (
        jnp.concatenate(
            [dust_pos, dust_vel, dust_tau[None, :], jnp.ones((1, per_device), jnp.float32)], axis=0
        )
        * live_rows[None, :]
    )
    outgoing = jnp.dot(
        dust_state, placing, precision=lax.Precision.HIGHEST, preferred_element_type=jnp.float32
    )
    wake_rows = jnp.concatenate([wake_pos, wake_gamma, wake_core[None, :]], axis=0)
    outgoing, wake_rows = lax.optimization_barrier((outgoing, wake_rows))
    arrived = exchange_slots(outgoing, capacity)
    region_wake = lax.all_gather(wake_rows, "narrow", axis=1, tiled=True)
    points = arrived[0:3]
    raw_sums = raw_terms(points, region_wake)
    return advance(arrived, raw_sums)


def solution(mesh):
    in_specs = (
        P(None, ("region", "narrow")),
        P(None, ("region", "narrow")),
        P(("region", "narrow")),
        P(("region", "narrow"), None),
        P(("region", "narrow")),
        P(None, ("region", "narrow")),
        P(None, ("region", "narrow")),
        P(("region", "narrow")),
    )
    out_specs = P(None, ("region", "narrow"))
    return jax.shard_map(body, mesh=mesh, in_specs=in_specs, out_specs=out_specs, check_vma=False)
```

profile of v0, /device:TPU:0, one launch (start us, length us, event | category | flops | bytes accessed | tf_op | source)
XLA Modules:
  0.0 33.0 jit_solution(9160325887394976063)
XLA Ops:
  0.0 0.9 %convert_reduce_fusion = s32[192]{0:T(256)S(1)} fusion(s32[192]{0:T(256)} %bitcast.62), kind=kLoop, calls=%fused_computation.34 | loop fusion | flops 184128 | bytes 1536 | tf_op jit(solution)/shard_map/reduce_sum | solution.py:105
  0.9 0.7 %multiply_add_fusion.1 = s32[192,1]{0,1:T(1,128)S(1)} fusion(s32[192,1]{0,1:T(1,128)S(1)} %bitcast.65, s32[192,1]{0,1:T(1,128)} %param.16), kind=kLoop, calls=%fused_computation.87 | loop fusion | flops 384 | bytes 2304 | tf_op jit(solution)/shard_map/add | solution.py:106
  2.3 0.1 pad.21.clone
  2.4 0.8 %pad_maximum_fusion = f32[7,1024]{1,0:T(8,128)S(1)} fusion(f32[1,1024]{1,0:T(1,128)} %bitcast.63, f32[3,1024]{1,0:T(4,128)} %param.19, f32[3,1024]{1,0:T(4,128)} %param.18), kind=kLoop, calls=%fused_computation.40 | loop fusion | flops 14336 | bytes 57344 | tf_op jit(solution)/shard_map/concatenate | solution.py:119
  3.1 1.0 %fusion.22 = f32[8,384]{1,0:T(8,128)S(1)} fusion(s32[192]{0:T(256)S(1)} %bitcast.69, f32[1,192]{1,0:T(1,128)} %bitcast.70, f32[3,192]{1,0:T(4,128)} %param.14, f32[3,192]{1,0:T(4,128)} %param.13, f32[8]{0:T(128)S(1)} %pad.21.clone, f32[192]{0:T(256)S(1)} %compare_convert_fusion), kind=kOutput, calls=%fused_computation.32 | convolution fusion | flops 7157760 | bytes 19232 | tf_op jit(solution)/shard_map/dot_general | solution.py:116
  4.1 0.1 reshape.132
  4.3 3.1 %collective-permute-start = (f32[8,96]{1,0:T(8,128)S(1)}, f32[8,96]{1,0:T(8,128)S(1)}, u32[]{:S(2)}, u32[]{:S(2)}) collective-permute-start(f32[8,96]{1,0:T(8,128)S(1)} %select_bitcast_fusion.2), channel_id=1, source_target_pairs={{0,8},{8,16},{16,24},{24,0},{1,9},{9,17},{17,25},{25,1},{2,10},{10... | collective-permute-start | bytes 9224 | tf_op jit(solution)/shard_map/ppermute | solution.py:90
  7.3 2.6 %collective-permute-start.1 = (f32[8,96]{1,0:T(8,128)S(1)}, f32[8,96]{1,0:T(8,128)S(1)}, u32[]{:S(2)}, u32[]{:S(2)}) collective-permute-start(f32[8,96]{1,0:T(8,128)S(1)} %select_bitcast_fusion.1), channel_id=1, source_target_pairs={{0,16},{8,24},{16,0},{24,8},{1,17},{9,25},{17,1},{25,9},{2,18},{10... | collective-permute-start | bytes 9224 | tf_op jit(solution)/shard_map/ppermute | solution.py:90
  9.9 1.3 %collective-permute-start.2 = (f32[8,96]{1,0:T(8,128)S(1)}, f32[8,96]{1,0:T(8,128)S(1)}, u32[]{:S(2)}, u32[]{:S(2)}) collective-permute-start(f32[8,96]{1,0:T(8,128)S(1)} %bitcast.64), channel_id=1, source_target_pairs={{0,24},{8,0},{16,8},{24,16},{1,25},{9,1},{17,9},{25,17},{2,26},{10... | collective-permute-start | bytes 9224 | tf_op jit(solution)/shard_map/ppermute | solution.py:90
  11.3 9.3 %all_gather.3 = f32[7,8192]{1,0:T(8,128)S(1)} all-gather(f32[7,1024]{1,0:T(8,128)S(1)} %pad_maximum_fusion), channel_id=1, replica_groups=mesh['region'=4,'narrow'=8] {'narrow'}, dimensions={1}, use_global_device_ids=true | all-gather | bytes 258048 | tf_op jit(solution)/shard_map/all_gather | solution.py:122
  20.6 0.3 fusion.25
  20.9 0.1 fusion.42
  21.0 0.1 maximum_bitcast_fusion
  21.1 0.0 collective-permute-done
  21.2 0.0 collective-permute-done.1
  21.2 0.0 collective-permute-done.2
  21.2 0.6 %gather_fusion = f32[4,8,96]{2,1,0:T(8,128)S(1)} fusion(f32[8,4,96]{2,0,1:T(8,128)S(1)} %pad_maximum_fusion.1, s32[1024]{0:T(1024)S(1)} %pad_clamp_fusion), kind=kCustom, calls=%fused_computation | custom fusion | bytes 24592 | tf_op jit(solution)/shard_map/jit(_take)/gather | solution.py:93
  21.8 0.1 select_bitcast_fusion
  21.9 0.1 slice.122
  22.0 0.0 copy-start
  22.0 9.7 %while.19 = (s32[]{:T(128)}, f32[6,384]{1,0:T(8,128)S(1)}, f32[4,6,2048]{2,1,0:T(8,128)S(1)}, f32[3,384]{1,0:T(4,128)S(1)}, f32[4,3,2048]{2,1,0:T(4,128)S(1)}, /...) while((s32[]{:T(128)}, f32[6,384]{1,0:T(8,128)S(1)}, ...), condition=%wide.region_2.4_spmd.clone, body=%wide.region_1.0_spmd.clone.sunk | while | flops 36966916 | bytes 200859 | solution.py:54
  22.1 2.3 %fusion.47 = f32[6,384]{1,0:T(8,128)S(1)} fusion(f32[2048]{0:T(1024)S(1)} %bitcast.55, f32[2048]{0:T(1024)S(1)} %bitcast.54, f32[384]{0:T(512)S(1)} %get-tuple-element.179, f32[2048]{0:T(1024)S(1)} %bitcast.53, f32[384]{0:T(512)S(1)} %get-tuple-element.181, f32[2048]{0:T(1024)S(1)} %bitcast.52, f32[384]{0:T(512)S(1)} %get-tuple-element.183, ...), kind=kOutput, calls=%fused_computation.20.clone.1 | convolution fusion | flops 36966912 | bytes 125957 | tf_op jit(solution)/shard_map/while/body/eval_jaxpr/while/body/eval_jaxpr/dot_general | solution.py:49
  24.4 0.1 constant_dynamic-slice_fusion.10
  24.5 2.3 %fusion.47 = f32[6,384]{1,0:T(8,128)S(1)} fusion(f32[2048]{0:T(1024)S(1)} %bitcast.55, f32[2048]{0:T(1024)S(1)} %bitcast.54, f32[384]{0:T(512)S(1)} %get-tuple-element.179, f32[2048]{0:T(1024)S(1)} %bitcast.53, f32[384]{0:T(512)S(1)} %get-tuple-element.181, f32[2048]{0:T(1024)S(1)} %bitcast.52, f32[384]{0:T(512)S(1)} %get-tuple-element.183, ...), kind=kOutput, calls=%fused_computation.20.clone.1 | convolution fusion | flops 36966912 | bytes 125957 | tf_op jit(solution)/shard_map/while/body/eval_jaxpr/while/body/eval_jaxpr/dot_general | solution.py:49
  26.8 0.1 constant_dynamic-slice_fusion.10
  27.0 2.3 %fusion.47 = f32[6,384]{1,0:T(8,128)S(1)} fusion(f32[2048]{0:T(1024)S(1)} %bitcast.55, f32[2048]{0:T(1024)S(1)} %bitcast.54, f32[384]{0:T(512)S(1)} %get-tuple-element.179, f32[2048]{0:T(1024)S(1)} %bitcast.53, f32[384]{0:T(512)S(1)} %get-tuple-element.181, f32[2048]{0:T(1024)S(1)} %bitcast.52, f32[384]{0:T(512)S(1)} %get-tuple-element.183, ...), kind=kOutput, calls=%fused_computation.20.clone.1 | convolution fusion | flops 36966912 | bytes 125957 | tf_op jit(solution)/shard_map/while/body/eval_jaxpr/while/body/eval_jaxpr/dot_general | solution.py:49
  29.3 0.1 constant_dynamic-slice_fusion.10
  29.4 2.3 %fusion.47 = f32[6,384]{1,0:T(8,128)S(1)} fusion(f32[2048]{0:T(1024)S(1)} %bitcast.55, f32[2048]{0:T(1024)S(1)} %bitcast.54, f32[384]{0:T(512)S(1)} %get-tuple-element.179, f32[2048]{0:T(1024)S(1)} %bitcast.53, f32[384]{0:T(512)S(1)} %get-tuple-element.181, f32[2048]{0:T(1024)S(1)} %bitcast.52, f32[384]{0:T(512)S(1)} %get-tuple-element.183, ...), kind=kOutput, calls=%fused_computation.20.clone.1 | convolution fusion | flops 36966912 | bytes 125957 | tf_op jit(solution)/shard_map/while/body/eval_jaxpr/while/body/eval_jaxpr/dot_general | solution.py:49
  31.7 0.1 squeeze.24
  31.8 0.1 squeeze.25
  31.9 0.1 squeeze.26
  32.0 0.1 squeeze.30
  32.1 0.1 squeeze.31
  32.2 0.1 slice.124
  32.3 0.0 copy-done
  32.3 0.1 multiply_add_fusion
  32.4 0.6 %maximum_multiply_fusion = f32[6,384]{1,0:T(8,128)} fusion(f32[3,384]{1,0:T(4,128)S(1)} %get-tuple-element.114, f32[3,384]{1,0:T(4,128)S(1)} %get-tuple-element.113, f32[384]{0:T(512)S(1)} %squeeze.30), kind=kLoop, calls=%fused_computation.46 | loop fusion | flops 4608 | bytes 19968 | tf_op jit(solution)/shard_map/mul | solution.py:77
  (27 shorter events, 0.4 us)
Async XLA Ops:
  4.3 16.9 %collective-permute-start = (f32[8,96]{1,0:T(8,128)S(1)}, f32[8,96]{1,0:T(8,128)S(1)}, u32[]{:S(2)}, u32[]{:S(2)}) collective-permute-start(f32[8,96]{1,0:T(8,128)S(1)} %select_bitcast_fusion.2), channel_id=1, source_target_pairs={{0,8},{8,16},{16,24},{24,0},{1,9},{9,17},{17,25},{25,1},{2,10},{10... | collective-permute-start | bytes 9224 | tf_op jit(solution)/shard_map/ppermute | solution.py:90
  7.3 13.8 %collective-permute-start.1 = (f32[8,96]{1,0:T(8,128)S(1)}, f32[8,96]{1,0:T(8,128)S(1)}, u32[]{:S(2)}, u32[]{:S(2)}) collective-permute-start(f32[8,96]{1,0:T(8,128)S(1)} %select_bitcast_fusion.1), channel_id=1, source_target_pairs={{0,16},{8,24},{16,0},{24,8},{1,17},{9,25},{17,1},{25,9},{2,18},{10... | collective-permute-start | bytes 9224 | tf_op jit(solution)/shard_map/ppermute | solution.py:90
  9.9 11.2 %collective-permute-start.2 = (f32[8,96]{1,0:T(8,128)S(1)}, f32[8,96]{1,0:T(8,128)S(1)}, u32[]{:S(2)}, u32[]{:S(2)}) collective-permute-start(f32[8,96]{1,0:T(8,128)S(1)} %bitcast.64), channel_id=1, source_target_pairs={{0,24},{8,0},{16,8},{24,16},{1,25},{9,1},{17,9},{25,17},{2,26},{10... | collective-permute-start | bytes 9224 | tf_op jit(solution)/shard_map/ppermute | solution.py:90
  22.0 10.4 %copy-start = (f32[3]{0:T(128)S(1)}, f32[3]{0:T(128)}, u32[]{:S(2)}) copy-start(f32[3]{0:T(128)} %constant.129) | copy-start | bytes 40
where the time goes:
time: 33.5 us; the launch traced here: 33 us
  matrix products  10.2 us (30%)
  blocking collectives  9.32 us (28%)
  starting transfers between devices  7.01 us (21%)
  other arithmetic  3.64 us (11%)
  local copies, waits for them, and re-layouts  1.92 us (6%)
  between operations  0.83 us (2%)
    all_gather x1, blocking collectives, body(): region_wake = lax.all_gather(wake_rows, 'narrow', axis=1, tiled=True)  9.32 us
    dot_general x4, matrix products, accumulate(): lax.dot_general(table_part, kernel, (((1,), (1,)), ((), ())), precision=l...  9.21 us
    ppermute x3, starting transfers between devices, exchange_slots(): by_shift.append(lax.ppermute(sent, 'region', pairs))  7.01 us
    dot_general x1, matrix products, body(): jnp.dot(dust_state, placing, precision=lax.Precision.HIGHEST, preferred_e...  1 us
    reduce_sum x1, other arithmetic, body(): slot_rank = jnp.sum(earlier.astype(jnp.int32), axis=1)  0.93 us
    concatenate x1, other arithmetic, body(): jnp.concatenate([wake_pos, wake_gamma, wake_core[None, :]], axis=0)  0.77 us
    add x1, other arithmetic, body(): column = target * capacity + slot_rank  0.69 us
  transfers between devices with their start and end apart: 3, of which 0 were waited for; matrix products, arithmetic and copies ran while one was open for 2% of the time, Pallas kernels for 0%

commit v1 on v0

--- a/solution.py
+++ b/solution.py
@@ -119,7 +119,14 @@
     wake_rows = jnp.concatenate([wake_pos, wake_gamma, wake_core[None, :]], axis=0)
     outgoing, wake_rows = lax.optimization_barrier((outgoing, wake_rows))
     arrived = exchange_slots(outgoing, capacity)
-    region_wake = lax.all_gather(wake_rows, "narrow", axis=1, tiled=True)
+    ring = [wake_rows]
+    for hop in range(7):
+        ring.append(lax.ppermute(ring[-1], "narrow", [(dev, (dev + 1) % 8) for dev in range(8)]))
+    region_wake = jnp.roll(
+        jnp.concatenate(ring[::-1], axis=1),
+        (lax.axis_index("narrow") + 1) * ring[0].shape[1],
+        axis=1,
+    )
     points = arrived[0:3]
     raw_sums = raw_terms(points, region_wake)
     return advance(arrived, raw_sums)

time: 33.5 us -> 48.9 us (1.46)
  waiting for transfers between devices: 0.01 us -> 23.4 us
  blocking collectives: 9.32 us -> 0 us
  starting transfers between devices: 7.01 us -> 7.85 us
    ppermute x0 -> x7, waiting for transfers between devices: none -> 22 us  [body(): lax.ppermute(ring[-1], 'narrow', [(dev, (dev + 1) % 8) for dev in range(8)])]
    all_gather x1 -> x0, blocking collectives: 9.32 us -> none  [body(): region_wake = lax.all_gather(wake_rows, 'narrow', axis=1, tiled=True)]
    ppermute x3, waiting for transfers between devices: 0.01 us -> 1.36 us  [exchange_slots(): by_shift.append(lax.ppermute(sent, 'region', pairs))]
    ppermute x0 -> x7, starting transfers between devices: none -> 1.26 us  [body(): lax.ppermute(ring[-1], 'narrow', [(dev, (dev + 1) % 8) for dev in range(8)])]
  transfers between devices with their start and end apart: 3 -> 10, of which waited for: 0 -> 7; matrix products, arithmetic and copies ran while one was open for 2% -> 3% of each run, Pallas kernels for 0% -> 0%
where the time goes in v1:
time: 48.9 us; the launch traced here: 48.5 us
  waiting for transfers between devices  23.4 us (48%)
  matrix products  10.2 us (21%)
  starting transfers between devices  7.85 us (16%)
  other arithmetic  3.92 us (8%)
  local copies, waits for them, and re-layouts  2.04 us (4%)
  between operations  0.94 us (2%)
    ppermute x7, waiting for transfers between devices, body(): lax.ppermute(ring[-1], 'narrow', [(dev, (dev + 1) % 8) for dev in range(8)])  22 us
    dot_general x4, matrix products, accumulate(): lax.dot_general(table_part, kernel, (((1,), (1,)), ((), ())), precision=l...  9.21 us
    ppermute x3, starting transfers between devices, exchange_slots(): by_shift.append(lax.ppermute(sent, 'region', pairs))  6.59 us
    ppermute x3, waiting for transfers between devices, exchange_slots(): by_shift.append(lax.ppermute(sent, 'region', pairs))  1.36 us
    ppermute x7, starting transfers between devices, body(): lax.ppermute(ring[-1], 'narrow', [(dev, (dev + 1) % 8) for dev in range(8)])  1.26 us
    dot_general x1, matrix products, body(): jnp.dot(dust_state, placing, precision=lax.Precision.HIGHEST, preferred_e...  1 us
  transfers between devices with their start and end apart: 10, of which 7 were waited for; matrix products, arithmetic and copies ran while one was open for 3% of the time, Pallas kernels for 0%

profile of v1, /device:TPU:0, one launch (start us, length us, event | category | flops | bytes accessed | tf_op | source)
XLA Modules:
  0.0 48.5 jit_solution(3729931973681833967)
XLA Ops:
  0.0 0.9 %convert_reduce_fusion = s32[192]{0:T(256)S(1)} fusion(s32[192]{0:T(256)} %bitcast.62), kind=kLoop, calls=%fused_computation.34 | loop fusion | flops 184128 | bytes 1536 | tf_op jit(solution)/shard_map/reduce_sum | solution.py:105
  0.9 0.7 %multiply_add_fusion.1 = s32[192,1]{0,1:T(1,128)S(1)} fusion(s32[192,1]{0,1:T(1,128)S(1)} %bitcast.65, s32[192,1]{0,1:T(1,128)} %param.16), kind=kLoop, calls=%fused_computation.107 | loop fusion | flops 384 | bytes 2304 | tf_op jit(solution)/shard_map/add | solution.py:106
  2.3 0.1 pad.21.clone
  2.4 0.8 %pad_maximum_fusion = f32[7,1024]{1,0:T(8,128)S(1)} fusion(f32[1,1024]{1,0:T(1,128)} %bitcast.63, f32[3,1024]{1,0:T(4,128)} %param.19, f32[3,1024]{1,0:T(4,128)} %param.18), kind=kLoop, calls=%fused_computation.40 | loop fusion | flops 14336 | bytes 57344 | tf_op jit(solution)/shard_map/concatenate | solution.py:119
  3.1 1.0 %fusion.22 = f32[8,384]{1,0:T(8,128)S(1)} fusion(s32[192]{0:T(256)S(1)} %bitcast.69, f32[1,192]{1,0:T(1,128)} %bitcast.70, f32[3,192]{1,0:T(4,128)} %param.14, f32[3,192]{1,0:T(4,128)} %param.13, f32[8]{0:T(128)S(1)} %pad.21.clone, f32[192]{0:T(256)S(1)} %compare_convert_fusion), kind=kOutput, calls=%fused_computation.32 | convolution fusion | flops 7157760 | bytes 19232 | tf_op jit(solution)/shard_map/dot_general | solution.py:116
  4.1 0.5 collective-permute-start.3
  4.6 0.1 reshape.132
  4.7 2.7 %collective-permute-start = (f32[8,96]{1,0:T(8,128)S(1)}, f32[8,96]{1,0:T(8,128)S(1)}, u32[]{:S(2)}, u32[]{:S(2)}) collective-permute-start(f32[8,96]{1,0:T(8,128)S(1)} %select_bitcast_fusion.2), channel_id=1, source_target_pairs={{0,8},{8,16},{16,24},{24,0},{1,9},{9,17},{17,25},{25,1},{2,10},{10... | collective-permute-start | bytes 9224 | tf_op jit(solution)/shard_map/ppermute | solution.py:90
  7.4 2.6 %collective-permute-start.1 = (f32[8,96]{1,0:T(8,128)S(1)}, f32[8,96]{1,0:T(8,128)S(1)}, u32[]{:S(2)}, u32[]{:S(2)}) collective-permute-start(f32[8,96]{1,0:T(8,128)S(1)} %select_bitcast_fusion.1), channel_id=1, source_target_pairs={{0,16},{8,24},{16,0},{24,8},{1,17},{9,25},{17,1},{25,9},{2,18},{10... | collective-permute-start | bytes 9224 | tf_op jit(solution)/shard_map/ppermute | solution.py:90
  10.0 1.3 %collective-permute-start.2 = (f32[8,96]{1,0:T(8,128)S(1)}, f32[8,96]{1,0:T(8,128)S(1)}, u32[]{:S(2)}, u32[]{:S(2)}) collective-permute-start(f32[8,96]{1,0:T(8,128)S(1)} %bitcast.64), channel_id=1, source_target_pairs={{0,24},{8,0},{16,8},{24,16},{1,25},{9,1},{17,9},{25,17},{2,26},{10... | collective-permute-start | bytes 9224 | tf_op jit(solution)/shard_map/ppermute | solution.py:90
  11.4 0.0 collective-permute-done.3
  11.4 0.8 %collective-permute-start.4 = (f32[7,1024]{1,0:T(8,128)S(1)}, f32[7,1024]{1,0:T(8,128)S(1)}, u32[]{:S(2)}, u32[]{:S(2)}) collective-permute-start(f32[7,1024]{1,0:T(8,128)S(1)} %collective-permute-done.3), channel_id=1, source_target_pairs={{0,1},{1,2},{2,3},{3,4},{4,5},{5,6},{6,7},{7,0},{8,9},{9,10},{10,1... | collective-permute-start | bytes 86024 | tf_op jit(solution)/shard_map/ppermute | solution.py:124
  12.2 0.0 collective-permute-done
  12.2 0.0 collective-permute-done.1
  12.2 1.4 %collective-permute-done.2 = f32[8,96]{1,0:T(8,128)S(1)} collective-permute-done((f32[8,96]{1,0:T(8,128)S(1)}, f32[8,96]{1,0:T(8,128)S(1)}, u32[]{:S(2)}, u32[]{:S(2)}) %collective-permute-start.2) | collective-permute-done | bytes 3104 | tf_op jit(solution)/shard_map/ppermute | solution.py:90
  13.6 0.5 %gather_fusion = f32[4,8,96]{2,1,0:T(8,128)S(1)} fusion(f32[8,4,96]{2,0,1:T(8,128)S(1)} %pad_maximum_fusion.1, s32[1024]{0:T(1024)S(1)} %pad_clamp_fusion), kind=kCustom, calls=%fused_computation | custom fusion | bytes 24592 | tf_op jit(solution)/shard_map/jit(_take)/gather | solution.py:93
  14.1 1.6 %collective-permute-done.4 = f32[7,1024]{1,0:T(8,128)S(1)} collective-permute-done((f32[7,1024]{1,0:T(8,128)S(1)}, f32[7,1024]{1,0:T(8,128)S(1)}, u32[]{:S(2)}, u32[]{:S(2)}) %collective-permute-start.4) | collective-permute-done | bytes 28704 | tf_op jit(solution)/shard_map/ppermute | solution.py:124
  15.7 0.0 collective-permute-start.5
  15.7 0.1 select_bitcast_fusion
  15.8 4.2 %collective-permute-done.5 = f32[7,1024]{1,0:T(8,128)S(1)} collective-permute-done((f32[7,1024]{1,0:T(8,128)S(1)}, f32[7,1024]{1,0:T(8,128)S(1)}, u32[]{:S(2)}, u32[]{:S(2)}) %collective-permute-start.5) | collective-permute-done | bytes 28704 | tf_op jit(solution)/shard_map/ppermute | solution.py:124
  19.9 0.0 collective-permute-start.6
  20.0 4.2 %collective-permute-done.6 = f32[7,1024]{1,0:T(8,128)S(1)} collective-permute-done((f32[7,1024]{1,0:T(8,128)S(1)}, f32[7,1024]{1,0:T(8,128)S(1)}, u32[]{:S(2)}, u32[]{:S(2)}) %collective-permute-start.6) | collective-permute-done | bytes 28704 | tf_op jit(solution)/shard_map/ppermute | solution.py:124
  24.2 0.0 collective-permute-start.7
  24.2 0.1 squeeze.30
  24.3 0.1 squeeze.31
  24.4 4.0 %collective-permute-done.7 = f32[7,1024]{1,0:T(8,128)S(1)} collective-permute-done((f32[7,1024]{1,0:T(8,128)S(1)}, f32[7,1024]{1,0:T(8,128)S(1)}, u32[]{:S(2)}, u32[]{:S(2)}) %collective-permute-start.7) | collective-permute-done | bytes 28704 | tf_op jit(solution)/shard_map/ppermute | solution.py:124
  28.4 0.0 collective-permute-start.8
  28.4 4.2 %collective-permute-done.8 = f32[7,1024]{1,0:T(8,128)S(1)} collective-permute-done((f32[7,1024]{1,0:T(8,128)S(1)}, f32[7,1024]{1,0:T(8,128)S(1)}, u32[]{:S(2)}, u32[]{:S(2)}) %collective-permute-start.8) | collective-permute-done | bytes 28704 | tf_op jit(solution)/shard_map/ppermute | solution.py:124
  32.7 0.0 collective-permute-start.9
  32.7 0.1 slice.122
  32.8 0.1 squeeze.24
  32.8 0.1 squeeze.25
  32.9 0.1 squeeze.26
  33.0 0.1 slice.124
  33.1 3.8 %collective-permute-done.9 = f32[7,1024]{1,0:T(8,128)S(1)} collective-permute-done((f32[7,1024]{1,0:T(8,128)S(1)}, f32[7,1024]{1,0:T(8,128)S(1)}, u32[]{:S(2)}, u32[]{:S(2)}) %collective-permute-start.9) | collective-permute-done | bytes 28704 | tf_op jit(solution)/shard_map/ppermute | solution.py:124
  37.1 0.1 constant_dynamic-slice_fusion.4
  37.2 0.5 %fusion.25 = (f32[8192]{0:T(1024)S(1)}, f32[1,8192]{1,0:T(1,128)S(1)}, f32[1,8192]{1,0:T(1,128)S(1)}, f32[1,8192]{1,0:T(1,128)S(1)}) fusion(f32[7,16384]{1,0:T(8,128)S(1)} %constant_dynamic-update-slice_fusion, s32[]{:T(128)S(6)} %add.167, s32[]{:T(128)S(6)} %select_n.90, s32[]{:T(128)S(6)} %add.165, s32[]{:T(128)S(6)} %add.164, s32[]{:T(128)S(6)} %add.163, ...), kind=kLoop, calls=%fused_computation.39 | loop fusion | flops 81920 | bytes 360476 | tf_op jit(solution)/shard_map/mul | solution.py:27
  37.8 0.1 maximum_bitcast_fusion
  37.9 0.0 copy-start
  37.9 9.8 %while.19 = (s32[]{:T(128)}, f32[6,384]{1,0:T(8,128)S(1)}, f32[4,6,2048]{2,1,0:T(8,128)S(1)}, f32[3,384]{1,0:T(4,128)S(1)}, f32[4,3,2048]{2,1,0:T(4,128)S(1)}, /...) while((s32[]{:T(128)}, f32[6,384]{1,0:T(8,128)S(1)}, ...), condition=%wide.region_2.4_spmd.clone, body=%wide.region_1.0_spmd.clone.sunk | while | flops 36966916 | bytes 200859 | solution.py:54
  38.0 2.3 %fusion.46 = f32[6,384]{1,0:T(8,128)S(1)} fusion(f32[2048]{0:T(1024)S(1)} %bitcast.55, f32[2048]{0:T(1024)S(1)} %bitcast.54, f32[384]{0:T(512)S(1)} %get-tuple-element.179, f32[2048]{0:T(1024)S(1)} %bitcast.53, f32[384]{0:T(512)S(1)} %get-tuple-element.181, f32[2048]{0:T(1024)S(1)} %bitcast.52, f32[384]{0:T(512)S(1)} %get-tuple-element.183, ...), kind=kOutput, calls=%fused_computation.20.clone.1 | convolution fusion | flops 36966912 | bytes 125957 | tf_op jit(solution)/shard_map/while/body/eval_jaxpr/while/body/eval_jaxpr/dot_general | solution.py:49
  40.3 0.1 constant_dynamic-slice_fusion.11
  40.5 2.3 %fusion.46 = f32[6,384]{1,0:T(8,128)S(1)} fusion(f32[2048]{0:T(1024)S(1)} %bitcast.55, f32[2048]{0:T(1024)S(1)} %bitcast.54, f32[384]{0:T(512)S(1)} %get-tuple-element.179, f32[2048]{0:T(1024)S(1)} %bitcast.53, f32[384]{0:T(512)S(1)} %get-tuple-element.181, f32[2048]{0:T(1024)S(1)} %bitcast.52, f32[384]{0:T(512)S(1)} %get-tuple-element.183, ...), kind=kOutput, calls=%fused_computation.20.clone.1 | convolution fusion | flops 36966912 | bytes 125957 | tf_op jit(solution)/shard_map/while/body/eval_jaxpr/while/body/eval_jaxpr/dot_general | solution.py:49
  42.8 0.1 constant_dynamic-slice_fusion.11
  42.9 2.3 %fusion.46 = f32[6,384]{1,0:T(8,128)S(1)} fusion(f32[2048]{0:T(1024)S(1)} %bitcast.55, f32[2048]{0:T(1024)S(1)} %bitcast.54, f32[384]{0:T(512)S(1)} %get-tuple-element.179, f32[2048]{0:T(1024)S(1)} %bitcast.53, f32[384]{0:T(512)S(1)} %get-tuple-element.181, f32[2048]{0:T(1024)S(1)} %bitcast.52, f32[384]{0:T(512)S(1)} %get-tuple-element.183, ...), kind=kOutput, calls=%fused_computation.20.clone.1 | convolution fusion | flops 36966912 | bytes 125957 | tf_op jit(solution)/shard_map/while/body/eval_jaxpr/while/body/eval_jaxpr/dot_general | solution.py:49
  45.2 0.1 constant_dynamic-slice_fusion.11
  45.4 2.3 %fusion.46 = f32[6,384]{1,0:T(8,128)S(1)} fusion(f32[2048]{0:T(1024)S(1)} %bitcast.55, f32[2048]{0:T(1024)S(1)} %bitcast.54, f32[384]{0:T(512)S(1)} %get-tuple-element.179, f32[2048]{0:T(1024)S(1)} %bitcast.53, f32[384]{0:T(512)S(1)} %get-tuple-element.181, f32[2048]{0:T(1024)S(1)} %bitcast.52, f32[384]{0:T(512)S(1)} %get-tuple-element.183, ...), kind=kOutput, calls=%fused_computation.20.clone.1 | convolution fusion | flops 36966912 | bytes 125957 | tf_op jit(solution)/shard_map/while/body/eval_jaxpr/while/body/eval_jaxpr/dot_general | solution.py:49
  47.7 0.1 multiply_subtract_fusion.5
  47.8 0.0 copy-done
  47.8 0.1 multiply_add_fusion
  47.8 0.6 %maximum_multiply_fusion = f32[6,384]{1,0:T(8,128)} fusion(f32[3,384]{1,0:T(4,128)S(1)} %get-tuple-element.114, f32[3,384]{1,0:T(4,128)S(1)} %get-tuple-element.113, f32[384]{0:T(512)S(1)} %squeeze.30), kind=kLoop, calls=%fused_computation.62 | loop fusion | flops 4608 | bytes 19968 | tf_op jit(solution)/shard_map/mul | solution.py:77
  (42 shorter events, 0.4 us)
Async XLA Ops:
  4.1 7.3 %collective-permute-start.3 = (f32[7,1024]{1,0:T(8,128)S(1)}, f32[7,1024]{1,0:T(8,128)S(1)}, u32[]{:S(2)}, u32[]{:S(2)}) collective-permute-start(f32[7,1024]{1,0:T(8,128)S(1)} %pad_maximum_fusion), channel_id=1, source_target_pairs={{0,1},{1,2},{2,3},{3,4},{4,5},{5,6},{6,7},{7,0},{8,9},{9,10},{10,1... | collective-permute-start | bytes 86024 | tf_op jit(solution)/shard_map/ppermute | solution.py:124
  4.7 7.5 %collective-permute-start = (f32[8,96]{1,0:T(8,128)S(1)}, f32[8,96]{1,0:T(8,128)S(1)}, u32[]{:S(2)}, u32[]{:S(2)}) collective-permute-start(f32[8,96]{1,0:T(8,128)S(1)} %select_bitcast_fusion.2), channel_id=1, source_target_pairs={{0,8},{8,16},{16,24},{24,0},{1,9},{9,17},{17,25},{25,1},{2,10},{10... | collective-permute-start | bytes 9224 | tf_op jit(solution)/shard_map/ppermute | solution.py:90
  7.4 4.8 %collective-permute-start.1 = (f32[8,96]{1,0:T(8,128)S(1)}, f32[8,96]{1,0:T(8,128)S(1)}, u32[]{:S(2)}, u32[]{:S(2)}) collective-permute-start(f32[8,96]{1,0:T(8,128)S(1)} %select_bitcast_fusion.1), channel_id=1, source_target_pairs={{0,16},{8,24},{16,0},{24,8},{1,17},{9,25},{17,1},{25,9},{2,18},{10... | collective-permute-start | bytes 9224 | tf_op jit(solution)/shard_map/ppermute | solution.py:90
  10.0 3.6 %collective-permute-start.2 = (f32[8,96]{1,0:T(8,128)S(1)}, f32[8,96]{1,0:T(8,128)S(1)}, u32[]{:S(2)}, u32[]{:S(2)}) collective-permute-start(f32[8,96]{1,0:T(8,128)S(1)} %bitcast.64), channel_id=1, source_target_pairs={{0,24},{8,0},{16,8},{24,16},{1,25},{9,1},{17,9},{25,17},{2,26},{10... | collective-permute-start | bytes 9224 | tf_op jit(solution)/shard_map/ppermute | solution.py:90
  11.4 4.3 %collective-permute-start.4 = (f32[7,1024]{1,0:T(8,128)S(1)}, f32[7,1024]{1,0:T(8,128)S(1)}, u32[]{:S(2)}, u32[]{:S(2)}) collective-permute-start(f32[7,1024]{1,0:T(8,128)S(1)} %collective-permute-done.3), channel_id=1, source_target_pairs={{0,1},{1,2},{2,3},{3,4},{4,5},{5,6},{6,7},{7,0},{8,9},{9,10},{10,1... | collective-permute-start | bytes 86024 | tf_op jit(solution)/shard_map/ppermute | solution.py:124
  15.7 4.2 %collective-permute-start.5 = (f32[7,1024]{1,0:T(8,128)S(1)}, f32[7,1024]{1,0:T(8,128)S(1)}, u32[]{:S(2)}, u32[]{:S(2)}) collective-permute-start(f32[7,1024]{1,0:T(8,128)S(1)} %collective-permute-done.4), channel_id=1, source_target_pairs={{0,1},{1,2},{2,3},{3,4},{4,5},{5,6},{6,7},{7,0},{8,9},{9,10},{10,1... | collective-permute-start | bytes 86024 | tf_op jit(solution)/shard_map/ppermute | solution.py:124
  19.9 4.2 %collective-permute-start.6 = (f32[7,1024]{1,0:T(8,128)S(1)}, f32[7,1024]{1,0:T(8,128)S(1)}, u32[]{:S(2)}, u32[]{:S(2)}) collective-permute-start(f32[7,1024]{1,0:T(8,128)S(1)} %collective-permute-done.5), channel_id=1, source_target_pairs={{0,1},{1,2},{2,3},{3,4},{4,5},{5,6},{6,7},{7,0},{8,9},{9,10},{10,1... | collective-permute-start | bytes 86024 | tf_op jit(solution)/shard_map/ppermute | solution.py:124
  24.2 4.2 %collective-permute-start.7 = (f32[7,1024]{1,0:T(8,128)S(1)}, f32[7,1024]{1,0:T(8,128)S(1)}, u32[]{:S(2)}, u32[]{:S(2)}) collective-permute-start(f32[7,1024]{1,0:T(8,128)S(1)} %collective-permute-done.6), channel_id=1, source_target_pairs={{0,1},{1,2},{2,3},{3,4},{4,5},{5,6},{6,7},{7,0},{8,9},{9,10},{10,1... | collective-permute-start | bytes 86024 | tf_op jit(solution)/shard_map/ppermute | solution.py:124
  28.4 4.2 %collective-permute-start.8 = (f32[7,1024]{1,0:T(8,128)S(1)}, f32[7,1024]{1,0:T(8,128)S(1)}, u32[]{:S(2)}, u32[]{:S(2)}) collective-permute-start(f32[7,1024]{1,0:T(8,128)S(1)} %collective-permute-done.7), channel_id=1, source_target_pairs={{0,1},{1,2},{2,3},{3,4},{4,5},{5,6},{6,7},{7,0},{8,9},{9,10},{10,1... | collective-permute-start | bytes 86024 | tf_op jit(solution)/shard_map/ppermute | solution.py:124
  32.7 4.2 %collective-permute-start.9 = (f32[7,1024]{1,0:T(8,128)S(1)}, f32[7,1024]{1,0:T(8,128)S(1)}, u32[]{:S(2)}, u32[]{:S(2)}) collective-permute-start(f32[7,1024]{1,0:T(8,128)S(1)} %collective-permute-done.8), channel_id=1, source_target_pairs={{0,1},{1,2},{2,3},{3,4},{4,5},{5,6},{6,7},{7,0},{8,9},{9,10},{10,1... | collective-permute-start | bytes 86024 | tf_op jit(solution)/shard_map/ppermute | solution.py:124
  37.9 9.9 %copy-start = (f32[3]{0:T(128)S(1)}, f32[3]{0:T(128)}, u32[]{:S(2)}) copy-start(f32[3]{0:T(128)} %constant.155) | copy-start | bytes 40
